TPU v7x, 256 devices: a whole 4x4x8 slice. The times are simulated.
256 devices in a mesh: clu: 32 (over x, z), grp: 8 (over y, core).
Axes of the slice: x: 4, y: 4, z: 8, core: 2. Of those that a mesh axis runs over, the one named last changes fastest.
Arguments:
- tokens: bfloat16 [262144, 1024], P(('clu', 'grp')), may hold values from -6 to 6
- segment_ids: int32 [256, 1024], P(('clu', 'grp')), may hold values from 0 to 127, never falling along the last dimension, each value on 1 to 32 neighbouring positions
- w_in: bfloat16 [1024, 2048], replicated, may hold values from -0.1875 to 0.1875
- b_in: float32 [2048], replicated, may hold values from -4 to 4
- w_out: bfloat16 [2048, 1024], replicated, may hold values from -0.125 to 0.125
- b_out: float32 [1024], replicated, may hold values from -1.5 to 1.5
- owner_ids: int32 [32768, 1], P(('clu', 'grp')), may hold values from 0 to 31; in each aligned block of 128 rows (0 to 127, 128 to 255, ...) at most 8 rows name the same one
- sub_ids: int32 [32768], P(('clu', 'grp')), may hold values from 0 to 511
Outputs:
- pooled: bfloat16 [32768, 1024], P(('clu', 'grp'))
- nearest: float32 [32768], P(('clu', 'grp'))
Inputs may be any that keep to these rules, and one draw needn't show every extreme that they name: `owner_ids`: no device holds more than 8 documents of one owner; some device holds exactly 8. `segment_ids`: each row lists documents 0 to 127 in order, each on 1 to 32 consecutive positions, one on exactly 32.
All inputs are finite; a program needn't handle non-finite values.
Results may differ from a plain program's by a relative error of at most 0.0043.
Values may be sent and summed in bfloat16 or wider, within the bound.
No kernel may reach another device: no remote copies, remote signals or barrier semaphores. Data moves between devices by JAX's collectives and lax.ppermute only.
A program may use at most 64 MiB of HBM per device.

v0:
```python
import jax
import jax.numpy as jnp
from jax import lax
from jax.sharding import PartitionSpec as P


def encode(token_block, segments, w_in, b_in, w_out, b_out, doc_count):
    pre_act = jnp.dot(token_block, w_in, preferred_element_type=jnp.float32) + b_in
    activated = jax.nn.gelu(pre_act, approximate=False).astype(jnp.bfloat16)
    layer_out = (
        token_block.astype(jnp.float32)
        + jnp.dot(activated, w_out, preferred_element_type=jnp.float32)
        + b_out
    ).astype(jnp.bfloat16)
    member = segments[None, :] == jnp.arange(doc_count, dtype=jnp.int32)[:, None]
    totals = jnp.dot(member.astype(jnp.bfloat16), layer_out, preferred_element_type=jnp.float32)
    counts = jnp.sum(member.astype(jnp.float32), axis=1, keepdims=True)
    mean_rows = totals / counts
    scale_inv = lax.rsqrt(jnp.sum(mean_rows * mean_rows, axis=1, keepdims=True) + 1e-06)
    return (mean_rows.astype(jnp.bfloat16), (mean_rows * scale_inv).astype(jnp.bfloat16))


def absorb(best_sim, own_units, own_meta, piece_units, piece_meta):
    similar = lax.dot_general(
        own_units, piece_units, (((1,), (1,)), ((), ())), preferred_element_type=jnp.float32
    )
    own_key = own_meta[:, 1][:, None]
    matched = (
        (own_key == piece_meta[:, 1][None, :])
        & (own_key >= 0)
        & (own_meta[:, 0][:, None] != piece_meta[:, 0][None, :])
    )
    return jnp.maximum(best_sim, jnp.max(jnp.where(matched, similar, -1.0), axis=1))


def per_device(tokens, segment_ids, w_in, b_in, w_out, b_out, owner_ids, sub_ids):
    n_clu = lax.axis_size("clu")
    n_grp = lax.axis_size("grp")
    doc_count = owner_ids.shape[0]
    model_width = tokens.shape[1]
    capacity = 2 * doc_count // n_clu
    own_count = n_clu * capacity
    pooled, unit_rows = encode(tokens, segment_ids[0], w_in, b_in, w_out, b_out, doc_count)
    owner_rank = owner_ids[:, 0]
    owner_hits = (owner_rank[:, None] == jnp.arange(n_clu, dtype=jnp.int32)[None, :]).astype(
        jnp.int32
    )
    before = jnp.cumsum(owner_hits, axis=0) - owner_hits
    slot_index = jnp.sum(before * owner_hits, axis=1)
    slot_place = owner_rank * capacity + slot_index
    grp_index = lax.axis_index("grp")
    device_rank = lax.axis_index("clu") * n_grp + grp_index
    doc_index = device_rank * doc_count + jnp.arange(doc_count, dtype=jnp.int32)
    start_best = jnp.full((own_count,), -1.0, jnp.float32)
    doc_info = jnp.stack([slot_place, doc_index, sub_ids], axis=1)
    every_unit, every_info = (
        lax.all_gather(unit_rows, "grp", axis=0, tiled=True),
        lax.all_gather(doc_info, "grp", axis=0, tiled=True),
    )
    source_grp = jnp.arange(n_grp * doc_count, dtype=jnp.int32) // doc_count
    wide_place = (
        every_info[:, 0] // capacity * (n_grp * capacity)
        + source_grp * capacity
        + every_info[:, 0] % capacity
    )
    send_units = (
        jnp.zeros((n_clu * n_grp * capacity, model_width), jnp.bfloat16)
        .at[wide_place]
        .set(every_unit)
    )
    send_meta = (
        jnp.full((n_clu * n_grp * capacity, 2), -1, jnp.int32).at[wide_place].set(every_info[:, 1:])
    )
    got_units, got_meta = (
        lax.all_to_all(
            send_units.reshape(n_clu, n_grp * capacity, model_width),
            "clu",
            split_axis=0,
            concat_axis=0,
            tiled=True,
        ),
        lax.all_to_all(
            send_meta.reshape(n_clu, n_grp * capacity, 2),
            "clu",
            split_axis=0,
            concat_axis=0,
            tiled=True,
        ),
    )
    own_units = lax.dynamic_slice_in_dim(
        got_units.reshape(n_clu, n_grp, capacity, model_width), grp_index, 1, 1
    ).reshape(own_count, model_width)
    own_meta = lax.dynamic_slice_in_dim(
        got_meta.reshape(n_clu, n_grp, capacity, 2), grp_index, 1, 1
    ).reshape(own_count, 2)
    best_sim = absorb(
        start_best,
        own_units,
        own_meta,
        got_units.reshape(n_clu * n_grp * capacity, model_width),
        got_meta.reshape(n_clu * n_grp * capacity, 2),
    )
    returned = lax.all_to_all(
        best_sim.reshape(n_clu, capacity), "clu", split_axis=0, concat_axis=0, tiled=True
    )
    nearest = jnp.take(returned.reshape(own_count), slot_place)
    return (pooled, nearest)


def solution(mesh):
    in_specs = (
        P(("clu", "grp"), None),
        P(("clu", "grp"), None),
        P(),
        P(),
        P(),
        P(),
        P(("clu", "grp"), None),
        P(("clu", "grp")),
    )
    out_specs = (P(("clu", "grp"), None), P(("clu", "grp")))
    return jax.shard_map(
        per_device, mesh=mesh, in_specs=in_specs, out_specs=out_specs, check_vma=False
    )
```

profile of v0, /device:TPU:1, one launch (start us, length us, event | category | flops | bytes accessed | tf_op | source)
XLA Modules:
  0.0 217.7 jit_solution(3338972314123578086)
XLA Ops:
  7.2 0.0 all-gather.2.cloned.1.call-start
  7.2 0.8 convert_reduce_fusion
  8.0 0.0 copy-start
  8.0 0.0 copy-start.1
  8.0 0.0 copy-start.3
  8.1 30.1 %fusion.10 = f32[1024,1024]{1,0:T(8,128)} fusion(bf16[2048,1024]{1,0:T(8,128)(2,1)} %param.12, f32[2048]{0:T(1024)} %param.11, bf16[1024,1024]{1,0:T(8,128)(2,1)} %param.8, bf16[1024,2048]{1,0:T(8,128)(2,1)} %param.10), kind=kOutput, calls=%fused_computation.23 | convolution fusion | flops 8728346624 | bytes 14688256 | tf_op jit(solution)/shard_map/dot_general | solution.py:12
  38.2 0.0 copy-done
  38.2 0.0 copy-done.1
  38.2 0.0 copy-done.3
  38.2 0.0 copy-start.2
  38.2 0.0 copy-start.4
  38.2 3.1 %multiply_reduce_fusion = (f32[128]{0:T(128)S(1)}, f32[128,1024]{1,0:T(8,128)S(1)}) fusion(f32[128]{0:T(128)S(1)} %convert_reduce_fusion, f32[1024,1024]{1,0:T(8,128)} %fusion.10, bf16[1024,1024]{1,0:T(8,128)(2,1)S(1)} %copy-done, f32[1024]{0:T(1024)S(1)} %copy-done.3, s32[1024]{0:T(1024)S(1)} %bitcast.43), kind=kOutput, calls=%fused_computation.35 | convolution fusion | flops 273153920 | bytes 6824960 | tf_op jit(solution)/shard_map/dot_general | solution.py:16
  41.3 0.8 multiply_convert_fusion
  42.1 0.0 all-gather.2.cloned.1.call-update
  42.2 0.0 copy-done.2
  42.2 0.1 fusion.25
  42.3 0.2 reduce_window_sum.11
  42.4 0.2 select_reduce_fusion
  42.6 0.0 copy-done.4
  42.6 14.5 %all_gather.6 = s32[1024,3]{0,1:T(4,128)S(1)} all-gather(s32[128,3]{0,1:T(4,128)S(1)} %pad_add_fusion), channel_id=1, replica_groups=mesh['clu'=32,'grp'=8] {'grp'}, dimensions={0}, use_global_device_ids=true | all-gather | bytes 13824 | tf_op jit(solution)/shard_map/all_gather | solution.py:58
  57.2 0.2 copy.28
  57.5 3.3 %scatter_custom_fusion = s32[2048,2]{1,0:T(8,128)S(1)} fusion(s32[1024]{0:T(1024)S(1)} %bitcast.48, s32[1024,2]{1,0:T(8,128)S(1)} %copy.28, s32[]{:T(128)} %constant.133.clone.1), kind=kCustom, calls=%fused_computation.36 | custom fusion | bytes 16388 | tf_op jit(solution)/shard_map/scatter | solution.py:72
  60.8 0.4 copy.29
  61.2 0.7 reshape.157
  61.9 10.2 %all-to-all-start = ((s32[32,1,128]{2,1,0:T(1,128)}), s32[32,1,128]{2,1,0:T(1,128)S(1)}, u32[]{:S(2)}, u32[]{:S(2)}) async-start(s32[32,1,128]{2,1,0:T(1,128)} %reshape.157), calls=%async_computation | async-start | bytes 32768 | tf_op jit(solution)/shard_map/all_to_all | solution.py:82
  72.2 2.2 %all-gather.2.cloned.1.call-done = bf16[1024,1024]{1,0:T(8,128)(2,1)} async-done(((bf16[128,1024]{1,0:T(8,128)(2,1)}), bf16[1024,1024]{1,0:T(8,128)(2,1)}) %all-gather.2.cloned.1.call-update) | async-done | bytes 2097168 | tf_op jit(solution)/shard_map/all_gather | solution.py:57
  74.4 8.6 %scatter_custom_fusion.1 = bf16[2048,1024]{1,0:T(8,128)(2,1)} fusion(s32[1024]{0:T(1024)S(1)} %bitcast.49, bf16[1024,1024]{1,0:T(8,128)(2,1)} %all-gather.2.cloned.1.call-done, bf16[]{:T(256)} %constant.144.clone.1), kind=kCustom, calls=%fused_computation.27 | custom fusion | bytes 4194816 | tf_op jit(solution)/shard_map/scatter | solution.py:69
  82.9 0.0 all-to-all-done
  82.9 9.7 %all-to-all-start.1 = ((bf16[32,64,1024]{2,1,0:T(8,128)(2,1)}), bf16[32,64,1024]{2,1,0:T(8,128)(2,1)}, u32[]{:S(2)}, u32[]{:S(2)}) async-start(bf16[32,64,1024]{2,1,0:T(8,128)(2,1)} %bitcast.36), calls=%async_computation.1 | async-start | bytes 8388608 | tf_op jit(solution)/shard_map/all_to_all | solution.py:75
  92.6 0.5 broadcast.140
  93.1 0.7 reduce.6
  93.8 0.1 reshape.158
  93.9 0.1 copy.30
  94.0 0.1 copy.31
  94.1 0.1 reshape.112
  94.2 0.1 reshape.113
  94.3 92.6 %all-to-all-done.1 = bf16[32,64,1024]{2,1,0:T(8,128)(2,1)} async-done(((bf16[32,64,1024]{2,1,0:T(8,128)(2,1)}), bf16[32,64,1024]{2,1,0:T(8,128)(2,1)}, u32[]{:S(2)}, u32[]{:S(2)}) %all-to-all-start.1) | async-done | bytes 4194336 | tf_op jit(solution)/shard_map/all_to_all | solution.py:75
  186.9 4.0 %fusion.18 = f32[256]{0:T(256)S(1)} fusion(bf16[2048,1024]{1,0:T(8,128)(2,1)} %bitcast.15, s32[2048]{0:T(1024)S(1)} %bitcast.45, s32[2048]{0:T(1024)S(1)} %bitcast.44, s32[256]{0:T(256)S(1)} %bitcast.51, s32[256]{0:T(256)S(1)} %bitcast.50, pred[256]{0:T(512)(128)(4,1)S(1)} %compare_reduce_fusion, bf16[32,8,8,1024]{3,2,1,0:T(8,128)(2,1)} %bitcast.13, ...), kind=kOutput, calls=%fused_computation.30 | convolution fusion | flops 1076887296 | bytes 4738308 | tf_op jit(solution)/shard_map/dot_general | solution.py:24
  190.9 0.7 max_broadcast_in_dim.15
  191.6 7.5 %all-to-all-start.2 = ((f32[32,1,8]{2,1,0:T(1,128)}), f32[32,1,8]{2,1,0:T(1,128)S(1)}, u32[]{:S(2)}, u32[]{:S(2)}) async-start(f32[32,1,8]{2,1,0:T(1,128)} %bitcast.16), calls=%async_computation.2 | async-start | bytes 32768 | tf_op jit(solution)/shard_map/all_to_all | solution.py:103
  199.2 8.6 %all-to-all-done.2 = f32[32,1,8]{2,1,0:T(1,128)S(1)} async-done(((f32[32,1,8]{2,1,0:T(1,128)}), f32[32,1,8]{2,1,0:T(1,128)S(1)}, u32[]{:S(2)}, u32[]{:S(2)}) %all-to-all-start.2) | async-done | bytes 1056 | tf_op jit(solution)/shard_map/all_to_all | solution.py:103
  207.8 0.5 broadcast.139
  208.3 0.7 reduce.5
  209.0 0.1 reshape.118
  209.1 1.3 gather_fusion
  210.4 0.5 bitcast_select_fusion
  (12 shorter events, 0.1 us)
Async XLA Ops:
  7.2 67.2 %all-gather.2.cloned.1.call-start = ((), (), s32[]{:S(2)}) async-start(), calls=%async_computation.3 | async-start | bytes 2359296 | tf_op jit(solution)/shard_map/all_gather | solution.py:57
  8.0 30.1 %copy-start = (bf16[1024,1024]{1,0:T(8,128)(2,1)S(1)}, bf16[1024,1024]{1,0:T(8,128)(2,1)}, u32[]{:S(2)}) copy-start(bf16[1024,1024]{1,0:T(8,128)(2,1)} %param.8) | copy-start | bytes 6291460
  8.0 30.1 %copy-start.1 = (s32[1,1024]{1,0:T(1,128)S(1)}, s32[1,1024]{1,0:T(1,128)}, u32[]{:S(2)}) copy-start(s32[1,1024]{1,0:T(1,128)} %param.9) | copy-start | bytes 12292
  8.0 30.1 %copy-start.3 = (f32[1024]{0:T(1024)S(1)}, f32[1024]{0:T(1024)}, u32[]{:S(2)}) copy-start(f32[1024]{0:T(1024)} %param.13) | copy-start | bytes 12292
  38.2 4.0 %copy-start.2 = (s32[128,1]{0,1:T(1,128)S(1)}, s32[128,1]{0,1:T(1,128)}, u32[]{:S(2)}) copy-start(s32[128,1]{0,1:T(1,128)} %param.14) | copy-start | bytes 1540
  38.2 4.4 %copy-start.4 = (s32[128]{0:T(128)S(1)}, s32[128]{0:T(128)}, u32[]{:S(2)}) copy-start(s32[128]{0:T(128)} %param.15) | copy-start | bytes 1540
  61.9 21.0 %all-to-all-start = ((s32[32,1,128]{2,1,0:T(1,128)}), s32[32,1,128]{2,1,0:T(1,128)S(1)}, u32[]{:S(2)}, u32[]{:S(2)}) async-start(s32[32,1,128]{2,1,0:T(1,128)} %reshape.157), calls=%async_computation | async-start | bytes 32768 | tf_op jit(solution)/shard_map/all_to_all | solution.py:82
  82.9 104.0 %all-to-all-start.1 = ((bf16[32,64,1024]{2,1,0:T(8,128)(2,1)}), bf16[32,64,1024]{2,1,0:T(8,128)(2,1)}, u32[]{:S(2)}, u32[]{:S(2)}) async-start(bf16[32,64,1024]{2,1,0:T(8,128)(2,1)} %bitcast.36), calls=%async_computation.1 | async-start | bytes 8388608 | tf_op jit(solution)/shard_map/all_to_all | solution.py:75
  191.6 16.2 %all-to-all-start.2 = ((f32[32,1,8]{2,1,0:T(1,128)}), f32[32,1,8]{2,1,0:T(1,128)S(1)}, u32[]{:S(2)}, u32[]{:S(2)}) async-start(f32[32,1,8]{2,1,0:T(1,128)} %bitcast.16), calls=%async_computation.2 | async-start | bytes 32768 | tf_op jit(solution)/shard_map/all_to_all | solution.py:103
Sparse Core Ops, SparseCore 0:
  42.3 32.0 all-gather.1
where the time goes:
time: 218 us
  waiting for transfers between devices  103 us (47%)
  matrix products  37.2 us (17%)
  starting transfers between devices  27.5 us (13%)
  local copies, waits for them, and re-layouts  16.8 us (8%)
  blocking collectives  14.5 us (7%)
  between operations  14.2 us (7%)
  other arithmetic  4.08 us (2%)
    all_to_all x1, waiting for transfers between devices, per_device(): lax.all_to_all(send_units.reshape(n_clu, n_grp * capacity, model_width),...  92.6 us
    dot_general x1, matrix products, encode(): jnp.dot(activated, w_out, preferred_element_type=jnp.float32)  30.1 us
    all_gather x1, blocking collectives, per_device(): lax.all_gather(doc_info, 'grp', axis=0, tiled=True)  14.5 us
    all_to_all x1, starting transfers between devices, per_device(): lax.all_to_all(send_meta.reshape(n_clu, n_grp * capacity, 2), 'clu', spli...  10.2 us
    all_to_all x1, starting transfers between devices, per_device(): lax.all_to_all(send_units.reshape(n_clu, n_grp * capacity, model_width),...  9.67 us
    all_to_all x1, waiting for transfers between devices, per_device(): lax.all_to_all(best_sim.reshape(n_clu, capacity), 'clu', split_axis=0, co...  8.64 us
    scatter x1, local copies, waits for them, and re-layouts, per_device(): send_units = jnp.zeros((n_clu * n_grp * capacity, model_width), jnp.bfloa...  8.55 us
    all_to_all x1, starting transfers between devices, per_device(): lax.all_to_all(best_sim.reshape(n_clu, capacity), 'clu', split_axis=0, co...  7.54 us
  transfers between devices with their start and end apart: 4, of which 3 were waited for; matrix products, arithmetic and copies ran while one was open for 7% of the time, Pallas kernels for 0%

commit v1 on v0

--- a/solution.py
+++ b/solution.py
@@ -2,6 +2,12 @@
 import jax.numpy as jnp
 from jax import lax
 from jax.sharding import PartitionSpec as P
+
+
+def guide_words_for(state):
+    return jnp.concatenate(
+        lax.all_to_all(jnp.stack(lax.axis_size("grp") * [state], axis=0), "grp", 0, 0), axis=0
+    )
 
 
 def encode(token_block, segments, w_in, b_in, w_out, b_out, doc_count):
@@ -55,7 +61,7 @@
     doc_info = jnp.stack([slot_place, doc_index, sub_ids], axis=1)
     every_unit, every_info = (
         lax.all_gather(unit_rows, "grp", axis=0, tiled=True),
-        lax.all_gather(doc_info, "grp", axis=0, tiled=True),
+        guide_words_for(doc_info),
     )
     source_grp = jnp.arange(n_grp * doc_count, dtype=jnp.int32) // doc_count
     wide_place = (

time: 218 us -> 218 us (level)
  blocking collectives: 14.5 us -> 10.4 us
  waiting for transfers between devices: 103 us -> 107 us
    all_gather x1 -> x0, blocking collectives: 14.5 us -> none  [per_device(): lax.all_gather(doc_info, 'grp', axis=0, tiled=True)]
    all_to_all x0 -> x1, blocking collectives: none -> 10.4 us  [guide_words_for(): lax.all_to_all(jnp.stack(lax.axis_size('grp') * [state], axis=0), 'grp',...]
    all_gather x1, waiting for transfers between devices: 2.2 us -> 5.52 us  [per_device(): lax.all_gather(unit_rows, 'grp', axis=0, tiled=True)]
where the time goes in v1:
time: 218 us
  waiting for transfers between devices  107 us (49%)
  matrix products  37.2 us (17%)
  starting transfers between devices  28.3 us (13%)
  local copies, waits for them, and re-layouts  16.8 us (8%)
  between operations  14.2 us (7%)
  blocking collectives  10.4 us (5%)
  other arithmetic  4.08 us (2%)
    all_to_all x1, waiting for transfers between devices, per_device(): lax.all_to_all(send_units.reshape(n_clu, n_grp * capacity, model_width),...  92.6 us
    dot_general x1, matrix products, encode(): jnp.dot(activated, w_out, preferred_element_type=jnp.float32)  30.1 us
    all_to_all x1, starting transfers between devices, per_device(): lax.all_to_all(send_meta.reshape(n_clu, n_grp * capacity, 2), 'clu', spli...  11 us
    all_to_all x1, blocking collectives, guide_words_for(): lax.all_to_all(jnp.stack(lax.axis_size('grp') * [state], axis=0), 'grp',...  10.4 us
    all_to_all x1, starting transfers between devices, per_device(): lax.all_to_all(send_units.reshape(n_clu, n_grp * capacity, model_width),...  9.67 us
    all_to_all x1, waiting for transfers between devices, per_device(): lax.all_to_all(best_sim.reshape(n_clu, capacity), 'clu', split_axis=0, co...  8.64 us
    scatter x1, local copies, waits for them, and re-layouts, per_device(): send_units = jnp.zeros((n_clu * n_grp * capacity, model_width), jnp.bfloa...  8.55 us
    all_to_all x1, starting transfers between devices, per_device(): lax.all_to_all(best_sim.reshape(n_clu, capacity), 'clu', split_axis=0, co...  7.53 us
  transfers between devices with their start and end apart: 4, of which 3 were waited for; matrix products, arithmetic and copies ran while one was open for 7% of the time, Pallas kernels for 0%

profile of v1, /device:TPU:1, one launch (start us, length us, event | category | flops | bytes accessed | tf_op | source)
XLA Modules:
  0.0 217.7 jit_solution(15635832240464519657)
XLA Ops:
  7.2 0.0 all-gather.2.cloned.1.call-start
  7.2 0.8 convert_reduce_fusion
  8.0 0.0 copy-start
  8.0 0.0 copy-start.1
  8.0 0.0 copy-start.3
  8.1 30.1 %fusion.10 = f32[1024,1024]{1,0:T(8,128)} fusion(bf16[2048,1024]{1,0:T(8,128)(2,1)} %param.12, f32[2048]{0:T(1024)} %param.11, bf16[1024,1024]{1,0:T(8,128)(2,1)} %param.8, bf16[1024,2048]{1,0:T(8,128)(2,1)} %param.10), kind=kOutput, calls=%fused_computation.23 | convolution fusion | flops 8728346624 | bytes 14688256 | tf_op jit(solution)/shard_map/dot_general | solution.py:18
  38.2 0.0 copy-done
  38.2 0.0 copy-done.1
  38.2 0.0 copy-done.3
  38.2 0.0 copy-start.2
  38.2 0.0 copy-start.4
  38.2 3.1 %multiply_reduce_fusion = (f32[128]{0:T(128)S(1)}, f32[128,1024]{1,0:T(8,128)S(1)}) fusion(f32[128]{0:T(128)S(1)} %convert_reduce_fusion, f32[1024,1024]{1,0:T(8,128)} %fusion.10, bf16[1024,1024]{1,0:T(8,128)(2,1)S(1)} %copy-done, f32[1024]{0:T(1024)S(1)} %copy-done.3, s32[1024]{0:T(1024)S(1)} %bitcast.46), kind=kOutput, calls=%fused_computation.35 | convolution fusion | flops 273153920 | bytes 6824960 | tf_op jit(solution)/shard_map/dot_general | solution.py:22
  41.3 0.8 multiply_convert_fusion
  42.1 0.0 all-gather.2.cloned.1.call-update
  42.2 0.0 copy-done.2
  42.2 0.1 fusion.25
  42.3 0.2 reduce_window_sum.11
  42.4 0.2 select_reduce_fusion
  42.6 0.0 copy-done.4
  42.7 10.4 %all_to_all.21 = s32[8,128,3]{1,2,0:T(4,128)S(1)} all-to-all(s32[8,128,3]{1,2,0:T(4,128)S(1)} %stack.8), channel_id=1, replica_groups=mesh['clu'=32,'grp'=8] {'grp'}, dimensions={0} | all-to-all | bytes 24576 | tf_op jit(solution)/shard_map/all_to_all | solution.py:9
  53.1 0.2 copy.25
  53.4 3.3 %scatter_custom_fusion = s32[2048,2]{1,0:T(8,128)S(1)} fusion(s32[1024]{0:T(1024)S(1)} %bitcast.51, s32[1024,2]{1,0:T(8,128)S(1)} %copy.25, s32[]{:T(128)} %constant.133.clone.1), kind=kCustom, calls=%fused_computation.36 | custom fusion | bytes 16388 | tf_op jit(solution)/shard_map/scatter | solution.py:78
  56.7 0.4 copy.26
  57.1 0.7 reshape.163
  57.8 11.0 %all-to-all-start.1 = ((s32[32,1,128]{2,1,0:T(1,128)}), s32[32,1,128]{2,1,0:T(1,128)S(1)}, u32[]{:S(2)}, u32[]{:S(2)}) async-start(s32[32,1,128]{2,1,0:T(1,128)} %reshape.163), calls=%async_computation.1 | async-start | bytes 32768 | tf_op jit(solution)/shard_map/all_to_all | solution.py:88
  68.8 5.5 %all-gather.2.cloned.1.call-done = bf16[1024,1024]{1,0:T(8,128)(2,1)} async-done(((bf16[128,1024]{1,0:T(8,128)(2,1)}), bf16[1024,1024]{1,0:T(8,128)(2,1)}) %all-gather.2.cloned.1.call-update) | async-done | bytes 2097168 | tf_op jit(solution)/shard_map/all_gather | solution.py:63
  74.4 8.6 %scatter_custom_fusion.1 = bf16[2048,1024]{1,0:T(8,128)(2,1)} fusion(s32[1024]{0:T(1024)S(1)} %bitcast.52, bf16[1024,1024]{1,0:T(8,128)(2,1)} %all-gather.2.cloned.1.call-done, bf16[]{:T(256)} %constant.144.clone.1), kind=kCustom, calls=%fused_computation.27 | custom fusion | bytes 4194816 | tf_op jit(solution)/shard_map/scatter | solution.py:75
  82.9 0.0 all-to-all-done.1
  82.9 9.7 %all-to-all-start.2 = ((bf16[32,64,1024]{2,1,0:T(8,128)(2,1)}), bf16[32,64,1024]{2,1,0:T(8,128)(2,1)}, u32[]{:S(2)}, u32[]{:S(2)}) async-start(bf16[32,64,1024]{2,1,0:T(8,128)(2,1)} %bitcast.37), calls=%async_computation.2 | async-start | bytes 8388608 | tf_op jit(solution)/shard_map/all_to_all | solution.py:81
  92.6 0.5 broadcast.142
  93.1 0.7 reduce.6
  93.8 0.1 reshape.164
  93.9 0.1 copy.27
  94.0 0.1 copy.28
  94.1 0.1 reshape.118
  94.2 0.1 reshape.119
  94.3 92.6 %all-to-all-done.2 = bf16[32,64,1024]{2,1,0:T(8,128)(2,1)} async-done(((bf16[32,64,1024]{2,1,0:T(8,128)(2,1)}), bf16[32,64,1024]{2,1,0:T(8,128)(2,1)}, u32[]{:S(2)}, u32[]{:S(2)}) %all-to-all-start.2) | async-done | bytes 4194336 | tf_op jit(solution)/shard_map/all_to_all | solution.py:81
  186.9 4.0 %fusion.18 = f32[256]{0:T(256)S(1)} fusion(bf16[2048,1024]{1,0:T(8,128)(2,1)} %bitcast.16, s32[2048]{0:T(1024)S(1)} %bitcast.48, s32[2048]{0:T(1024)S(1)} %bitcast.47, s32[256]{0:T(256)S(1)} %bitcast.54, s32[256]{0:T(256)S(1)} %bitcast.53, pred[256]{0:T(512)(128)(4,1)S(1)} %compare_reduce_fusion, bf16[32,8,8,1024]{3,2,1,0:T(8,128)(2,1)} %bitcast.14, ...), kind=kOutput, calls=%fused_computation.30 | convolution fusion | flops 1076887296 | bytes 4738308 | tf_op jit(solution)/shard_map/dot_general | solution.py:30
  190.9 0.7 max_broadcast_in_dim.15
  191.6 7.5 %all-to-all-start.3 = ((f32[32,1,8]{2,1,0:T(1,128)}), f32[32,1,8]{2,1,0:T(1,128)S(1)}, u32[]{:S(2)}, u32[]{:S(2)}) async-start(f32[32,1,8]{2,1,0:T(1,128)} %bitcast.17), calls=%async_computation.3 | async-start | bytes 32768 | tf_op jit(solution)/shard_map/all_to_all | solution.py:109
  199.2 8.6 %all-to-all-done.3 = f32[32,1,8]{2,1,0:T(1,128)S(1)} async-done(((f32[32,1,8]{2,1,0:T(1,128)}), f32[32,1,8]{2,1,0:T(1,128)S(1)}, u32[]{:S(2)}, u32[]{:S(2)}) %all-to-all-start.3) | async-done | bytes 1056 | tf_op jit(solution)/shard_map/all_to_all | solution.py:109
  207.8 0.5 broadcast.141
  208.3 0.7 reduce.5
  209.0 0.1 reshape.124
  209.1 1.3 gather_fusion
  210.4 0.5 bitcast_select_fusion
  (13 shorter events, 0.1 us)
Async XLA Ops:
  7.2 67.2 %all-gather.2.cloned.1.call-start = ((), (), s32[]{:S(2)}) async-start(), calls=%async_computation.4 | async-start | bytes 2359296 | tf_op jit(solution)/shard_map/all_gather | solution.py:63
  8.0 30.1 %copy-start = (bf16[1024,1024]{1,0:T(8,128)(2,1)S(1)}, bf16[1024,1024]{1,0:T(8,128)(2,1)}, u32[]{:S(2)}) copy-start(bf16[1024,1024]{1,0:T(8,128)(2,1)} %param.8) | copy-start | bytes 6291460
  8.0 30.1 %copy-start.1 = (s32[1,1024]{1,0:T(1,128)S(1)}, s32[1,1024]{1,0:T(1,128)}, u32[]{:S(2)}) copy-start(s32[1,1024]{1,0:T(1,128)} %param.9) | copy-start | bytes 12292
  8.0 30.1 %copy-start.3 = (f32[1024]{0:T(1024)S(1)}, f32[1024]{0:T(1024)}, u32[]{:S(2)}) copy-start(f32[1024]{0:T(1024)} %param.13) | copy-start | bytes 12292
  38.2 4.0 %copy-start.2 = (s32[128,1]{0,1:T(1,128)S(1)}, s32[128,1]{0,1:T(1,128)}, u32[]{:S(2)}) copy-start(s32[128,1]{0,1:T(1,128)} %param.14) | copy-start | bytes 1540
  38.2 4.4 %copy-start.4 = (s32[128]{0:T(128)S(1)}, s32[128]{0:T(128)}, u32[]{:S(2)}) copy-start(s32[128]{0:T(128)} %param.15) | copy-start | bytes 1540
  57.8 25.1 %all-to-all-start.1 = ((s32[32,1,128]{2,1,0:T(1,128)}), s32[32,1,128]{2,1,0:T(1,128)S(1)}, u32[]{:S(2)}, u32[]{:S(2)}) async-start(s32[32,1,128]{2,1,0:T(1,128)} %reshape.163), calls=%async_computation.1 | async-start | bytes 32768 | tf_op jit(solution)/shard_map/all_to_all | solution.py:88
  82.9 104.0 %all-to-all-start.2 = ((bf16[32,64,1024]{2,1,0:T(8,128)(2,1)}), bf16[32,64,1024]{2,1,0:T(8,128)(2,1)}, u32[]{:S(2)}, u32[]{:S(2)}) async-start(bf16[32,64,1024]{2,1,0:T(8,128)(2,1)} %bitcast.37), calls=%async_computation.2 | async-start | bytes 8388608 | tf_op jit(solution)/shard_map/all_to_all | solution.py:81
  191.6 16.2 %all-to-all-start.3 = ((f32[32,1,8]{2,1,0:T(1,128)}), f32[32,1,8]{2,1,0:T(1,128)S(1)}, u32[]{:S(2)}, u32[]{:S(2)}) async-start(f32[32,1,8]{2,1,0:T(1,128)} %bitcast.17), calls=%async_computation.3 | async-start | bytes 32768 | tf_op jit(solution)/shard_map/all_to_all | solution.py:109
Sparse Core Ops, SparseCore 0:
  42.3 32.0 all-gather.1
